TPU v7x, 256 devices: a whole 4x4x8 slice. The times are simulated.
256 devices in a mesh: hours: 64 (over z_hi, x, y, core), blocks: 4 (over z_lo).
Axes of the slice: x: 4, y: 4, z: 8 (z_hi: 2, z_lo: 4; z = z_hi * 4 + z_lo), core: 2. Of those that a mesh axis runs over, the one named last changes fastest.
Arguments:
- spectra: float32 [64, 64, 3, 2, 2048], P('hours', 'blocks'), may hold values from -6 to 6
- validity: int32 [64, 64], P('hours', 'blocks'), may hold values from 0 to 1, as said below
Outputs:
- near_stack: float32 [4, 2, 2304, 256], P('blocks', None, 'hours')
- far_stack: float32 [4, 1152, 256], P('blocks', 'hours')
Inputs may be any that keep to these rules, and one draw needn't show every extreme that they name: `validity`: 0 or 1; some stations are invalid in every hour.
All inputs are finite; a program needn't handle non-finite values.
Results may differ from a plain program's by a relative error of at most 0.0058.
Values may be sent and summed in bfloat16 or wider, within the bound.
No kernel may reach another device: no remote copies, remote signals or barrier semaphores. Data moves between devices by JAX's collectives and lax.ppermute only.
A program may use at most 64 MiB of HBM per device.

v0:
```python
import math

import jax
import jax.numpy as jnp
from jax import lax
from jax.experimental import pallas as pl
from jax.experimental.pallas import tpu as pltpu
from jax.sharding import Mesh, PartitionSpec as P


BAND = 128
LAGS = 256


EPSILON = 1e-06


HOUR_AXES = ("z_hi", "x", "y", "core")
HOUR_SPLIT = (2, 4, 4, 2)
STACK_STEPS = 4


def passed_along(block, axis, distance):
    devices = range(lax.axis_size(axis))
    route = [((i - distance) % len(devices), i) for i in devices]
    return lax.ppermute(block, axis, route)


def whiten(spectra, validity, band_width):
    hour_count, station_count, comp_count, part_count, freq_count = spectra.shape
    grouped = spectra.reshape(
        hour_count, station_count, comp_count, part_count, freq_count // band_width, band_width
    )
    band_power = jnp.mean(grouped * grouped, axis=(3, 5), keepdims=True)
    valid_f = validity.astype(jnp.float32).reshape(hour_count, station_count, 1, 1, 1, 1)
    scaled = grouped * (valid_f / jnp.sqrt(band_power + EPSILON))
    return scaled.reshape(hour_count, station_count * comp_count, part_count, freq_count).astype(
        jnp.bfloat16
    )


def build_table(freq_count, lag_count):
    fine_count = 64
    coarse_count = freq_count // fine_count
    lag_index = jnp.arange(lag_count, dtype=jnp.int32)[None, :] - lag_count // 2
    period = 2 * freq_count

    def angle_of(freq_index):
        residue = freq_index[:, None] * (lag_index + period) % period
        return residue.astype(jnp.float32) * (math.pi / freq_count)

    coarse = angle_of(jnp.arange(coarse_count, dtype=jnp.int32) * fine_count)[:, None, :]
    fine = angle_of(jnp.arange(fine_count, dtype=jnp.int32))[None, :, :]
    coarse_cos, coarse_sin = jnp.cos(coarse), jnp.sin(coarse)
    fine_cos, fine_sin = jnp.cos(fine), jnp.sin(fine)
    cos_part = (coarse_cos * fine_cos - coarse_sin * fine_sin).reshape(freq_count, lag_count)
    sin_part = (coarse_sin * fine_cos + coarse_cos * fine_sin).reshape(freq_count, lag_count)
    amplitude = 8.0 / math.sqrt(freq_count)
    return jnp.concatenate([cos_part * amplitude, -sin_part * amplitude], 0).astype(jnp.bfloat16)


def cross_into(rows_ref, cols_ref, cross_ref):
    row_step = rows_ref.shape[1]
    col_count, wide = cols_ref.shape
    freq_count = wide // 2
    chunk = 256
    for start in range(0, freq_count, chunk):
        col_real = cols_ref[:, start : start + chunk].astype(jnp.float32)
        col_imag = cols_ref[:, freq_count + start : freq_count + start + chunk].astype(jnp.float32)
        for row in range(row_step):
            row_real = rows_ref[0, row : row + 1, start : start + chunk].astype(jnp.float32)
            row_imag = rows_ref[0, row : row + 1, freq_count + start : freq_count + start + chunk]
            row_imag = row_imag.astype(jnp.float32)
            real_part = row_real * col_real + row_imag * col_imag
            imag_part = row_imag * col_real - row_real * col_imag
            first = row * col_count
            cross_ref[first : first + col_count, start : start + chunk] = real_part.astype(jnp.bfloat16)
            cross_ref[first : first + col_count, freq_count + start : freq_count + start + chunk] = (
                imag_part.astype(jnp.bfloat16)
            )


def slot_rows(result, out_ref, offset, share):
    minor, major = out_ref.shape[:2]
    for slot in range(minor * major):
        out_ref[slot % minor, slot // minor, offset : offset + share, :] = result[
            slot * share : (slot + 1) * share
        ]


def correlated(rows_ref, cols_ref, table_ref, cross_ref):
    cross_into(rows_ref, cols_ref, cross_ref)
    return jnp.dot(cross_ref[...], table_ref[...], preferred_element_type=jnp.float32)


def own_kernel(near_rows_ref, own_ref, table_ref, out_ref, cross_ref):
    slots = out_ref.shape[0] * out_ref.shape[1]
    near_share = near_rows_ref.shape[1] * own_ref.shape[0] // slots
    slot_rows(correlated(near_rows_ref, own_ref, table_ref, cross_ref), out_ref, 0, near_share)
    out_ref[:, :, near_share:, :] = jnp.zeros(
        out_ref.shape[:2] + (out_ref.shape[2] - near_share, out_ref.shape[3]), jnp.float32
    )


def passed_kernel(
    near_rows_ref, passed_ref, far_rows_ref, far_cols_ref, table_ref, count_ref, after_ref,
    out_ref, near_cross_ref, far_cross_ref,
):
    slots = out_ref.shape[0] * out_ref.shape[1]
    near_share = near_rows_ref.shape[1] * passed_ref.shape[0] // slots
    far_share = far_rows_ref.shape[1] * far_cols_ref.shape[0] // slots
    result = correlated(near_rows_ref, passed_ref, table_ref, near_cross_ref)
    slot_rows(result, out_ref, 0, near_share)
    result = correlated(far_rows_ref, far_cols_ref, table_ref, far_cross_ref)
    slot_rows(result, out_ref, near_share, far_share)
    out_ref[:, :, near_share + far_share :, :] = count_ref[...]


def slot_array(kernel, inputs, in_specs, hour_devices, row_total, lag_count, scratch):
    steps = STACK_STEPS
    minor = HOUR_SPLIT[-1]
    major = hour_devices // minor
    return pl.pallas_call(
        kernel,
        grid=(steps,),
        in_specs=in_specs,
        out_specs=pl.BlockSpec((minor, major // steps, row_total, lag_count), lambda i: (0, i, 0, 0)),
        out_shape=jax.ShapeDtypeStruct((minor, major, row_total, lag_count), jnp.float32),
        scratch_shapes=scratch,
    )(*inputs)


def own_slots(white, table, hour_devices, row_total):
    trace_count, wide = white.shape
    lag_count = table.shape[1]
    near_step = trace_count // STACK_STEPS
    full = lambda i: (0, 0)
    in_specs = [
        pl.BlockSpec((1, near_step, wide), lambda i: (i, 0, 0)),
        pl.BlockSpec((trace_count, wide), full),
        pl.BlockSpec((wide, lag_count), full),
    ]
    inputs = (white.reshape(STACK_STEPS, near_step, wide), white, table)
    scratch = [pltpu.VMEM((near_step * trace_count, wide), jnp.bfloat16)]
    return slot_array(own_kernel, inputs, in_specs, hour_devices, row_total, lag_count, scratch)


def passed_slots(white, passed, far_rows, far_cols, table, count_tail, after, hour_devices, row_total):
    trace_count, wide = white.shape
    half_width = far_rows.shape[0]
    lag_count = table.shape[1]
    near_step = trace_count // STACK_STEPS
    far_step = half_width // STACK_STEPS
    minor = HOUR_SPLIT[-1]
    slots = hour_devices // STACK_STEPS
    full = lambda i: (0, 0)
    in_specs = [
        pl.BlockSpec((1, near_step, wide), lambda i: (i, 0, 0)),
        pl.BlockSpec((trace_count, wide), full),
        pl.BlockSpec((1, far_step, wide), lambda i: (i, 0, 0)),
        pl.BlockSpec((trace_count, wide), full),
        pl.BlockSpec((wide, lag_count), full),
        pl.BlockSpec((minor, slots // minor) + count_tail.shape[2:], lambda i: (0, i, 0, 0)),
        pl.BlockSpec(memory_space=pl.ANY),
    ]
    inputs = (
        white.reshape(STACK_STEPS, near_step, wide), passed,
        far_rows.reshape(STACK_STEPS, far_step, wide), far_cols, table, count_tail, after,
    )
    scratch = [
        pltpu.VMEM((near_step * trace_count, wide), jnp.bfloat16),
        pltpu.VMEM((far_step * trace_count, wide), jnp.bfloat16),
    ]
    return slot_array(passed_kernel, inputs, in_specs, hour_devices, row_total, lag_count, scratch)


def core_swap(block):
    core = lax.axis_index("core")
    kept = lax.dynamic_index_in_dim(block, core, 0, keepdims=False)
    sent = lax.dynamic_index_in_dim(block, 1 - core, 0, keepdims=False)
    return kept + lax.ppermute(sent, "core", [(0, 1), (1, 0)])


def on_device(spectra, validity):
    _, station_count, comp_count, part_count, freq_count = spectra.shape
    trace_count = station_count * comp_count
    half_width = trace_count // 2
    wide = part_count * freq_count
    white = whiten(spectra, validity, BAND).reshape(trace_count, wide)
    table = build_table(freq_count, LAGS)
    valid_wire = validity.astype(jnp.bfloat16)
    block_count = lax.axis_size("blocks")
    near_rounds = block_count // 2
    my_block = lax.axis_index("blocks")
    is_lower = my_block < near_rounds
    panels = [(white, valid_wire)]
    for round_index in range(1, near_rounds + 1):
        panels.append(passed_along((white, valid_wire), "blocks", round_index))
    far_white, far_valid = panels[near_rounds]
    far_rows = jnp.where(is_lower, white[:half_width], far_white[half_width:])
    far_cols = jnp.where(is_lower, far_white, white)

    def trace_valid(valid):
        return jnp.repeat(valid.reshape(-1).astype(jnp.float32), comp_count)

    own_valid = trace_valid(valid_wire)
    near_pairs = jnp.stack(
        [
            (own_valid[:, None] * trace_valid(panels[round_index][1])[None, :]).reshape(-1)
            for round_index in range(near_rounds)
        ],
        0,
    )
    far_trace_valid = trace_valid(far_valid)
    far_row_valid = jnp.where(is_lower, own_valid[:half_width], far_trace_valid[half_width:])
    far_col_valid = jnp.where(is_lower, far_trace_valid, own_valid)
    far_pairs = (far_row_valid[:, None] * far_col_valid[None, :]).reshape(-1)

    hour_devices = math.prod(HOUR_SPLIT)
    share_near = trace_count * trace_count // hour_devices
    share_far = half_width * trace_count // hour_devices
    lag_count = table.shape[1]
    count_slots = jnp.concatenate(
        [
            near_pairs.reshape(near_rounds, hour_devices, share_near).transpose(1, 0, 2).reshape(hour_devices, -1),
            far_pairs.reshape(hour_devices, share_far),
        ],
        1,
    )
    row_count = near_rounds * share_near + share_far
    first_rows = -(-share_near // 8) * 8
    rest_rows = -(-(row_count - share_near + 1) // 8) * 8
    count_tail = jnp.zeros((hour_devices, rest_rows - row_count + share_near, lag_count), jnp.float32)
    count_tail = count_tail.at[:, 0, :row_count].set(count_slots)
    minor = HOUR_SPLIT[-1]
    count_tail = count_tail.reshape((hour_devices // minor, minor) + count_tail.shape[1:])
    count_tail = count_tail.transpose(1, 0, 2, 3)
    own = own_slots(white, table, hour_devices, first_rows)
    first = core_swap(own)
    rest = passed_slots(white, panels[1][0], far_rows, far_cols, table, count_tail, own, hour_devices, rest_rows)
    total = jnp.concatenate([first, core_swap(rest)], 1)
    total = total.reshape((HOUR_SPLIT[0], -1) + total.shape[1:]).astype(jnp.bfloat16)
    incoming = lax.all_to_all(total, ("x", "y"), 1, 1, tiled=True)
    total = jnp.sum(incoming.astype(jnp.float32), axis=1)
    upper = lax.axis_index("z_hi") > 0
    kept = jnp.where(upper, total[1], total[0])
    sent = jnp.where(upper, total[0], total[1])
    total = kept + lax.ppermute(sent, "z_hi", [(0, 1), (1, 0)])
    count_at = first_rows + row_count - share_near
    pair_counts = jnp.maximum(total[count_at, :row_count], 1.0)
    first_stack = total[:share_near] / pair_counts[:share_near, None]
    rest_stack = total[first_rows:count_at] / pair_counts[share_near:, None]
    near_stack = jnp.concatenate([first_stack, rest_stack[: (near_rounds - 1) * share_near]], 0)
    near_stack = near_stack.reshape(near_rounds, share_near, lag_count)
    far_stack = rest_stack[(near_rounds - 1) * share_near :]
    return (near_stack[None], far_stack[None])


def solution(mesh):
    hour_mesh = Mesh(
        mesh.devices.reshape(HOUR_SPLIT + (mesh.shape["blocks"],)), HOUR_AXES + ("blocks",)
    )
    in_specs = (P(HOUR_AXES, "blocks", None, None, None), P(HOUR_AXES, "blocks"))
    out_specs = (P("blocks", None, HOUR_AXES, None), P("blocks", HOUR_AXES, None))
    return jax.shard_map(
        on_device, mesh=hour_mesh, in_specs=in_specs, out_specs=out_specs, check_vma=False
    )
```

profile of v0, /device:TPU:1, one launch (start us, length us, event | category | flops | bytes accessed | tf_op | source)
XLA Modules:
  0.0 108.9 jit_solution(12153974503822851700)
XLA Ops:
  0.6 0.7 convert_convert_fusion
  1.4 3.8 %collective-permute-start.4 = (bf16[1,16]{1,0:T(2,128)(2,1)S(1)}, bf16[1,16]{1,0:T(2,128)(2,1)S(1)}, u32[]{:S(2)}, u32[]{:S(2)}) collective-permute-start(bf16[1,16]{1,0:T(2,128)(2,1)S(1)} %get-tuple-element.30), channel_id=1, source_target_pairs={{2,0},{3,1},{0,2},{1,3},{6,4},{7,5},{4,6},{5,7},{10,8},{11,9},{8,1... | collective-permute-start | bytes 104 | tf_op jit(solution)/shard_map/ppermute | solution.py:26
  5.2 1.6 %collective-permute-start.3 = (bf16[1,16]{1,0:T(2,128)(2,1)S(1)}, bf16[1,16]{1,0:T(2,128)(2,1)S(1)}, u32[]{:S(2)}, u32[]{:S(2)}) collective-permute-start(bf16[1,16]{1,0:T(2,128)(2,1)S(1)} %get-tuple-element.30), channel_id=1, source_target_pairs={{3,0},{0,1},{1,2},{2,3},{7,4},{4,5},{5,6},{6,7},{11,8},{8,9},{9,10... | collective-permute-start | bytes 104 | tf_op jit(solution)/shard_map/ppermute | solution.py:26
  6.8 2.3 %multiply_reduce_fusion = f32[16,3,2048]{2,1,0:T(4,128)S(1)} fusion(f32[1,16,3,2,2048]{4,3,2,1,0:T(2,128)} %param.4), kind=kLoop, calls=%fused_computation.13 | loop fusion | flops 294912 | bytes 1179648 | tf_op jit(solution)/shard_map/reduce_sum | solution.py:34
  9.1 0.3 reshape.372
  9.4 0.2 reduce_sum.27
  9.7 0.2 mul.274
  9.8 0.1 copy.40
  10.0 0.4 mul.276
  10.4 0.5 copy.29
  10.9 0.5 copy.28
  11.4 0.1 collective-permute-start.2
  11.6 1.9 %collective-permute-start.1 = (bf16[48,4096]{1,0:T(8,128)(2,1)S(1)}, bf16[48,4096]{1,0:T(8,128)(2,1)}, u32[]{:S(2)}, u32[]{:S(2)}) collective-permute-start(bf16[48,4096]{1,0:T(8,128)(2,1)S(1)} %multiply_convert_fusion.3.own_ref), channel_id=1, source_target_pairs={{3,0},{0,1},{1,2},{2,3},{7,4},{4,5},{5,6},{6,7},{11,8},{8,9},{9,10... | collective-permute-start | bytes 1179656 | tf_op jit(solution)/shard_map/ppermute | solution.py:26
  13.5 0.7 mul.277
  14.1 1.6 %reshape.363 = f32[4,12,4096]{2,1,0:T(8,128)} reshape(f32[1,16,3,2,2048]{4,3,2,1,0:T(2,128)S(1)} %copy-done.1) | data formatting | bytes 1572864 | tf_op jit(solution)/shard_map/reshape | solution.py:31
  15.9 0.1 mul.307
  16.0 0.3 fusion.13
  16.2 0.2 fusion.18
  16.5 0.2 fusion.2
  16.8 0.8 multiply_convert_fusion.1
  17.5 1.5 %pad_maximum_fusion.table_ref = bf16[4096,256]{1,0:T(8,128)(2,1)} fusion(bf16[2048,256]{1,0:T(8,128)(2,1)S(1)} %bitcast.63, bf16[2048,256]{1,0:T(8,128)(2,1)S(1)} %bitcast.62), kind=kLoop, calls=%fused_computation.1 | loop fusion | flops 4194304 | bytes 4194304 | tf_op jit(solution)/shard_map/concatenate | solution.py:59
  19.0 0.1 copy-done.2
  19.1 1.0 multiply_convert_fusion.2.near_rows_ref
  20.1 8.3 %shard_map.41.after_ref = f32[2,32,40,256]{3,2,1,0:T(8,128)} custom-call(bf16[4,12,4096]{2,1,0:T(8,128)(2,1)} %multiply_convert_fusion.2.near_rows_ref, bf16[48,4096]{1,0:T(8,128)(2,1)} %copy-done.3, bf16[4096,256]{1,0:T(8,128)(2,1)} %pad_maximum_fusion.table_ref), custom_call_target="tpu_custom_call" | custom-call | tf_op jit(solution)/shard_map/pallas_call | solution.py:123
  28.5 0.1 reshape.368
  29.1 0.1 mul.312
  29.5 0.1 copy.18
  29.7 0.7 copy.41
  30.4 9.7 %collective-permute-done.2 = bf16[48,4096]{1,0:T(8,128)(2,1)} collective-permute-done((bf16[48,4096]{1,0:T(8,128)(2,1)S(1)}, bf16[48,4096]{1,0:T(8,128)(2,1)}, u32[]{:S(2)}, u32[]{:S(2)}) %collective-permute-start.2) | collective-permute-done | bytes 393248 | tf_op jit(solution)/shard_map/ppermute | solution.py:26
  40.2 1.8 %broadcast_select_fusion.far_cols_ref = bf16[48,4096]{1,0:T(8,128)(2,1)} fusion(bf16[48,4096]{1,0:T(8,128)(2,1)} %collective-permute-done.2, bf16[48,4096]{1,0:T(8,128)(2,1)S(1)} %copy-done.4, pred[]{:T(512)S(6)} %lt.33), kind=kLoop, calls=%fused_computation.17 | loop fusion | flops 196608 | bytes 1179649 | tf_op jit(solution)/shard_map/jit(_where)/select_n | solution.py:201
  41.9 0.9 slice_select_fusion
  42.9 0.8 reshape.366.far_rows_ref
  43.7 11.5 %shard_map.42 = f32[2,32,56,256]{3,2,1,0:T(8,128)} custom-call(bf16[4,12,4096]{2,1,0:T(8,128)(2,1)} %multiply_convert_fusion.2.near_rows_ref, bf16[48,4096]{1,0:T(8,128)(2,1)} %collective-permute-done.1.passed_ref, bf16[4,6,4096]{2,1,0:T(8,128)(2,1)} %reshape.366.far_rows_ref, bf16[48,4096]{1,0:T(8,128)(2,1)} %broadcast_select_fusion.far_cols_ref, ...), custom_call_target="tpu_custom_call" | custom-call | tf_op jit(solution)/shard_map/pallas_call | solution.py:123
  55.1 3.1 %dynamic-slice_bitcast_fusion = f32[32,56,256]{2,1,0:T(8,128)} fusion(f32[2,32,56,256]{3,2,1,0:T(8,128)} %shard_map.42, s32[]{:T(128)S(6)} %select_n.110), kind=kLoop, calls=%fused_computation.6 | loop fusion | bytes 3670020 | tf_op jit(solution)/shard_map/jit(dynamic_index_in_dim)/squeeze | solution.py:180
  58.2 0.5 collective-permute-start.5
  58.7 1.2 %dynamic-slice_bitcast_fusion.1 = f32[32,40,256]{2,1,0:T(8,128)} fusion(f32[2,32,40,256]{3,2,1,0:T(8,128)S(1)} %copy-done, s32[]{:T(128)S(6)} %select_n.110), kind=kLoop, calls=%fused_computation.10 | loop fusion | bytes 2621444 | tf_op jit(solution)/shard_map/jit(dynamic_index_in_dim)/squeeze | solution.py:180
  59.9 4.4 %collective-permute-done = f32[32,40,256]{2,1,0:T(8,128)} collective-permute-done((f32[32,40,256]{2,1,0:T(8,128)}, f32[32,40,256]{2,1,0:T(8,128)}, u32[]{:S(2)}, u32[]{:S(2)}) %collective-permute-start) | collective-permute-done | bytes 1310752 | tf_op jit(solution)/shard_map/ppermute | solution.py:181
  64.3 1.4 %fusion.1 = bf16[32,40,256]{2,1,0:T(8,128)(2,1)S(1)} fusion(f32[32,40,256]{2,1,0:T(8,128)} %collective-permute-done, f32[2,32,40,256]{3,2,1,0:T(8,128)S(1)} %copy-done, s32[]{:T(128)S(6)} %select_n.109), kind=kLoop, calls=%fused_computation.9 | loop fusion | flops 655360 | bytes 3276804 | tf_op jit(solution)/shard_map/convert.1
  65.8 2.2 %fusion = bf16[32,56,256]{2,1,0:T(8,128)(2,1)S(1)} fusion(f32[32,56,256]{2,1,0:T(8,128)} %collective-permute-done.5, f32[2,32,56,256]{3,2,1,0:T(8,128)} %shard_map.42, s32[]{:T(128)S(6)} %select_n.109), kind=kLoop, calls=%fused_computation.5 | loop fusion | flops 917504 | bytes 4587524 | tf_op jit(solution)/shard_map/convert.2
  68.0 0.2 pad_maximum_fusion.1
  68.2 1.3 %copy.22 = bf16[2,16,96,256]{3,2,0,1:T(8,128)(2,1)} copy(bf16[2,16,96,256]{3,2,1,0:T(8,128)(2,1)S(1)} %bitcast.61) | data formatting | bytes 3145728 | tf_op jit(solution)/shard_map/convert_element_type | solution.py:242
  69.5 6.8 %all-to-all-start = ((bf16[2,16,96,256]{3,2,0,1:T(8,128)(2,1)}), bf16[2,16,96,256]{3,2,0,1:T(8,128)(2,1)S(1)}, u32[]{:S(2)}, u32[]{:S(2)}) async-start(bf16[2,16,96,256]{3,2,0,1:T(8,128)(2,1)} %copy.22), calls=%async_computation | async-start | bytes 3145728 | tf_op jit(solution)/shard_map/all_to_all | solution.py:243
  76.3 22.3 %all-to-all-done = bf16[2,16,96,256]{3,2,0,1:T(8,128)(2,1)S(1)} async-done(((bf16[2,16,96,256]{3,2,0,1:T(8,128)(2,1)}), bf16[2,16,96,256]{3,2,0,1:T(8,128)(2,1)S(1)}, u32[]{:S(2)}, u32[]{:S(2)}) %all-to-all-start) | async-done | bytes 1572896 | tf_op jit(solution)/shard_map/all_to_all | solution.py:243
  98.5 0.2 convert_reduce_fusion
  98.8 4.6 %collective-permute-start.6 = (f32[96,256]{1,0:T(8,128)S(1)}, f32[96,256]{1,0:T(8,128)S(1)}, u32[]{:S(2)}, u32[]{:S(2)}) collective-permute-start(f32[96,256]{1,0:T(8,128)S(1)} %select_bitcast_fusion), channel_id=1, source_target_pairs={{0,128},{128,0},{1,129},{129,1},{2,130},{130,2},{3,131},{131,3},{4... | collective-permute-start | bytes 294920 | tf_op jit(solution)/shard_map/ppermute | solution.py:248
  103.3 3.9 %collective-permute-done.6 = f32[96,256]{1,0:T(8,128)S(1)} collective-permute-done((f32[96,256]{1,0:T(8,128)S(1)}, f32[96,256]{1,0:T(8,128)S(1)}, u32[]{:S(2)}, u32[]{:S(2)}) %collective-permute-start.6) | collective-permute-done | bytes 98336 | tf_op jit(solution)/shard_map/ppermute | solution.py:248
  107.6 0.7 copy.23
  108.3 0.6 broadcast_in_dim.14
  (52 shorter events, 1.7 us)
Async XLA Ops:
  1.4 27.0 %collective-permute-start.4 = (bf16[1,16]{1,0:T(2,128)(2,1)S(1)}, bf16[1,16]{1,0:T(2,128)(2,1)S(1)}, u32[]{:S(2)}, u32[]{:S(2)}) collective-permute-start(bf16[1,16]{1,0:T(2,128)(2,1)S(1)} %get-tuple-element.30), channel_id=1, source_target_pairs={{2,0},{3,1},{0,2},{1,3},{6,4},{7,5},{4,6},{5,7},{10,8},{11,9},{8,1... | collective-permute-start | bytes 104 | tf_op jit(solution)/shard_map/ppermute | solution.py:26
  5.2 23.9 %collective-permute-start.3 = (bf16[1,16]{1,0:T(2,128)(2,1)S(1)}, bf16[1,16]{1,0:T(2,128)(2,1)S(1)}, u32[]{:S(2)}, u32[]{:S(2)}) collective-permute-start(bf16[1,16]{1,0:T(2,128)(2,1)S(1)} %get-tuple-element.30), channel_id=1, source_target_pairs={{3,0},{0,1},{1,2},{2,3},{7,4},{4,5},{5,6},{6,7},{11,8},{8,9},{9,10... | collective-permute-start | bytes 104 | tf_op jit(solution)/shard_map/ppermute | solution.py:26
  9.6 1.3 %copy-start.1 = (f32[1,16,3,2,2048]{4,3,2,1,0:T(2,128)S(1)}, f32[1,16,3,2,2048]{4,3,2,1,0:T(2,128)}, u32[]{:S(2)}) copy-start(f32[1,16,3,2,2048]{4,3,2,1,0:T(2,128)} %param.4) | copy-start | bytes 2359300
  11.4 4.8 %copy-start.3 = (bf16[48,4096]{1,0:T(8,128)(2,1)}, bf16[48,4096]{1,0:T(8,128)(2,1)S(1)}, u32[]{:S(2)}) copy-start(bf16[48,4096]{1,0:T(8,128)(2,1)S(1)} %multiply_convert_fusion.3.own_ref) | copy-start | bytes 1179652
  11.4 28.7 %collective-permute-start.2 = (bf16[48,4096]{1,0:T(8,128)(2,1)S(1)}, bf16[48,4096]{1,0:T(8,128)(2,1)}, u32[]{:S(2)}, u32[]{:S(2)}) collective-permute-start(bf16[48,4096]{1,0:T(8,128)(2,1)S(1)} %multiply_convert_fusion.3.own_ref), channel_id=1, source_target_pairs={{2,0},{3,1},{0,2},{1,3},{6,4},{7,5},{4,6},{5,7},{10,8},{11,9},{8,1... | collective-permute-start | bytes 1179656 | tf_op jit(solution)/shard_map/ppermute | solution.py:26
  11.6 32.1 %collective-permute-start.1 = (bf16[48,4096]{1,0:T(8,128)(2,1)S(1)}, bf16[48,4096]{1,0:T(8,128)(2,1)}, u32[]{:S(2)}, u32[]{:S(2)}) collective-permute-start(bf16[48,4096]{1,0:T(8,128)(2,1)S(1)} %multiply_convert_fusion.3.own_ref), channel_id=1, source_target_pairs={{3,0},{0,1},{1,2},{2,3},{7,4},{4,5},{5,6},{6,7},{11,8},{8,9},{9,10... | collective-permute-start | bytes 1179656 | tf_op jit(solution)/shard_map/ppermute | solution.py:26
  17.5 1.6 %copy-start.2 = (f32[4,12,4096]{2,1,0:T(8,128)S(1)}, f32[4,12,4096]{2,1,0:T(8,128)}, u32[]{:S(2)}) copy-start(f32[4,12,4096]{2,1,0:T(8,128)} %reshape.363) | copy-start | bytes 2359300
  20.1 20.1 %copy-start.4 = (bf16[48,4096]{1,0:T(8,128)(2,1)S(1)}, bf16[48,4096]{1,0:T(8,128)(2,1)}, u32[]{:S(2)}) copy-start(bf16[48,4096]{1,0:T(8,128)(2,1)} %copy-done.3) | copy-start | bytes 1179652
  55.1 3.6 %copy-start = (f32[2,32,40,256]{3,2,1,0:T(8,128)S(1)}, f32[2,32,40,256]{3,2,1,0:T(8,128)}, u32[]{:S(2)}) copy-start(f32[2,32,40,256]{3,2,1,0:T(8,128)} %shard_map.41.after_ref) | copy-start | bytes 7864324
  58.2 7.6 %collective-permute-start.5 = (f32[32,56,256]{2,1,0:T(8,128)}, f32[32,56,256]{2,1,0:T(8,128)}, u32[]{:S(2)}, u32[]{:S(2)}) collective-permute-start(f32[32,56,256]{2,1,0:T(8,128)} %dynamic-slice_bitcast_fusion), channel_id=1, source_target_pairs={{0,4},{4,0},{1,5},{5,1},{2,6},{6,2},{3,7},{7,3},{8,12},{12,8},{9,1... | collective-permute-start | bytes 5505032 | tf_op jit(solution)/shard_map/ppermute | solution.py:181
  59.9 4.5 %collective-permute-start = (f32[32,40,256]{2,1,0:T(8,128)}, f32[32,40,256]{2,1,0:T(8,128)}, u32[]{:S(2)}, u32[]{:S(2)}) collective-permute-start(f32[32,40,256]{2,1,0:T(8,128)} %dynamic-slice_bitcast_fusion.1), channel_id=1, source_target_pairs={{0,4},{4,0},{1,5},{5,1},{2,6},{6,2},{3,7},{7,3},{8,12},{12,8},{9,1... | collective-permute-start | bytes 3932168 | tf_op jit(solution)/shard_map/ppermute | solution.py:181
  69.5 29.0 %all-to-all-start = ((bf16[2,16,96,256]{3,2,0,1:T(8,128)(2,1)}), bf16[2,16,96,256]{3,2,0,1:T(8,128)(2,1)S(1)}, u32[]{:S(2)}, u32[]{:S(2)}) async-start(bf16[2,16,96,256]{3,2,0,1:T(8,128)(2,1)} %copy.22), calls=%async_computation | async-start | bytes 3145728 | tf_op jit(solution)/shard_map/all_to_all | solution.py:243
  98.8 8.5 %collective-permute-start.6 = (f32[96,256]{1,0:T(8,128)S(1)}, f32[96,256]{1,0:T(8,128)S(1)}, u32[]{:S(2)}, u32[]{:S(2)}) collective-permute-start(f32[96,256]{1,0:T(8,128)S(1)} %select_bitcast_fusion), channel_id=1, source_target_pairs={{0,128},{128,0},{1,129},{129,1},{2,130},{130,2},{3,131},{131,3},{4... | collective-permute-start | bytes 294920 | tf_op jit(solution)/shard_map/ppermute | solution.py:248
where the time goes:
time: 111 us; the launch traced here: 109 us
  waiting for transfers between devices  40.4 us (36%)
  Pallas kernels  19.8 us (18%)
  starting transfers between devices  19.3 us (17%)
  other arithmetic  14.5 us (13%)
  local copies, waits for them, and re-layouts  13.9 us (13%)
    all_to_all x1, waiting for transfers between devices, on_device(): incoming = lax.all_to_all(total, ('x', 'y'), 1, 1, tiled=True)  22.3 us
    pallas_call x2, Pallas kernels, slot_array(): pl.pallas_call(kernel, grid=(steps,), in_specs=in_specs, out_specs=pl.Blo...  19.8 us
    ppermute x4, waiting for transfers between devices, passed_along(): return lax.ppermute(block, axis, route)  9.75 us
    ppermute x4, starting transfers between devices, passed_along(): return lax.ppermute(block, axis, route)  7.44 us
    all_to_all x1, starting transfers between devices, on_device(): incoming = lax.all_to_all(total, ('x', 'y'), 1, 1, tiled=True)  6.77 us
    ppermute x1, starting transfers between devices, on_device(): total = kept + lax.ppermute(sent, 'z_hi', [(0, 1), (1, 0)])  4.57 us
    another operation x4, other arithmetic  4.45 us
    ppermute x2, waiting for transfers between devices, core_swap(): return kept + lax.ppermute(sent, 'core', [(0, 1), (1, 0)])  4.44 us
  transfers between devices with their start and end apart: 8, of which 4 were waited for; matrix products, arithmetic and copies ran while one was open for 17% of the time, Pallas kernels for 8%

commit v1 on v0

--- a/solution.py
+++ b/solution.py
@@ -193,9 +193,12 @@
     near_rounds = block_count // 2
     my_block = lax.axis_index("blocks")
     is_lower = my_block < near_rounds
+    valid_rows = jnp.zeros((8, wide), jnp.bfloat16).at[0, :station_count].set(valid_wire.reshape(-1))
+    packed = jnp.concatenate([white, valid_rows], 0)
     panels = [(white, valid_wire)]
     for round_index in range(1, near_rounds + 1):
-        panels.append(passed_along((white, valid_wire), "blocks", round_index))
+        panel = passed_along(packed, "blocks", round_index)
+        panels.append((panel[:trace_count], panel[trace_count, :station_count]))
     far_white, far_valid = panels[near_rounds]
     far_rows = jnp.where(is_lower, white[:half_width], far_white[half_width:])
     far_cols = jnp.where(is_lower, far_white, white)

time: 111 us -> 117 us (1.054)
  other arithmetic: 14.5 us -> 17.7 us
  local copies, waits for them, and re-layouts: 13.9 us -> 16.3 us
    ppermute x4 -> x2, starting transfers between devices: 7.44 us -> 5.45 us  [passed_along(): return lax.ppermute(block, axis, route)]
    ppermute x1, waiting for transfers between devices: 3.95 us -> 2.01 us  [on_device(): total = kept + lax.ppermute(sent, 'z_hi', [(0, 1), (1, 0)])]
    ppermute x4 -> x2, waiting for transfers between devices: 9.75 us -> 11.6 us  [passed_along(): return lax.ppermute(block, axis, route)]
    ppermute x1, starting transfers between devices: 4.57 us -> 6.36 us  [on_device(): total = kept + lax.ppermute(sent, 'z_hi', [(0, 1), (1, 0)])]
    slice x0 -> x1, local copies, waits for them, and re-layouts: none -> 1.76 us  [on_device(): panels.append((panel[:trace_count], panel[trace_count, :station_count]))]
    ppermute x2, starting transfers between devices: 0.51 us -> 1.86 us  [core_swap(): return kept + lax.ppermute(sent, 'core', [(0, 1), (1, 0)])]
    convert_element_type x3, other arithmetic: 0.74 us -> 2.09 us  [trace_valid(): return jnp.repeat(valid.reshape(-1).astype(jnp.float32), comp_count)]
  transfers between devices with their start and end apart: 8 -> 6, of which waited for: 4 -> 4; matrix products, arithmetic and copies ran while one was open for 17% -> 10% of each run, Pallas kernels for 8% -> 7%
where the time goes in v1:
time: 117 us; the launch traced here: 115 us
  waiting for transfers between devices  40.3 us (34%)
  starting transfers between devices  20.4 us (17%)
  Pallas kernels  19.7 us (17%)
  other arithmetic  17.7 us (15%)
  local copies, waits for them, and re-layouts  16.3 us (14%)
    all_to_all x1, waiting for transfers between devices, on_device(): incoming = lax.all_to_all(total, ('x', 'y'), 1, 1, tiled=True)  22.3 us
    pallas_call x2, Pallas kernels, slot_array(): pl.pallas_call(kernel, grid=(steps,), in_specs=in_specs, out_specs=pl.Blo...  19.7 us
    ppermute x2, waiting for transfers between devices, passed_along(): return lax.ppermute(block, axis, route)  11.6 us
    all_to_all x1, starting transfers between devices, on_device(): incoming = lax.all_to_all(total, ('x', 'y'), 1, 1, tiled=True)  6.75 us
    ppermute x1, starting transfers between devices, on_device(): total = kept + lax.ppermute(sent, 'z_hi', [(0, 1), (1, 0)])  6.36 us
    ppermute x2, starting transfers between devices, passed_along(): return lax.ppermute(block, axis, route)  5.45 us
    ppermute x2, waiting for transfers between devices, core_swap(): return kept + lax.ppermute(sent, 'core', [(0, 1), (1, 0)])  4.46 us
    another operation x4, other arithmetic  4.45 us
  transfers between devices with their start and end apart: 6, of which 4 were waited for; matrix products, arithmetic and copies ran while one was open for 10% of the time, Pallas kernels for 7%

profile of v1, /device:TPU:1, one launch (start us, length us, event | category | flops | bytes accessed | tf_op | source)
XLA Modules:
  0.0 115.3 jit_solution(17278599101922102700)
XLA Ops:
  0.6 0.7 convert_convert_fusion
  1.4 2.3 %multiply_reduce_fusion = f32[16,3,2048]{2,1,0:T(4,128)S(1)} fusion(f32[1,16,3,2,2048]{4,3,2,1,0:T(2,128)} %param.6), kind=kLoop, calls=%fused_computation.15 | loop fusion | flops 294912 | bytes 1179648 | tf_op jit(solution)/shard_map/reduce_sum | solution.py:34
  3.6 0.3 reshape.399
  3.9 0.2 reduce_sum.27
  4.2 0.2 mul.274
  4.4 0.1 copy.40
  4.5 0.4 mul.276
  5.0 0.5 copy.29
  5.4 0.5 copy.28
  6.0 0.9 fusion.3
  6.9 3.8 %collective-permute-start.2 = (bf16[56,4096]{1,0:T(8,128)(2,1)}, bf16[56,4096]{1,0:T(8,128)(2,1)}, u32[]{:S(2)}, u32[]{:S(2)}) collective-permute-start(bf16[56,4096]{1,0:T(8,128)(2,1)} %fusion.3), channel_id=1, source_target_pairs={{2,0},{3,1},{0,2},{1,3},{6,4},{7,5},{4,6},{5,7},{10,8},{11,9},{8,1... | collective-permute-start | bytes 1376264 | tf_op jit(solution)/shard_map/ppermute | solution.py:26
  10.7 1.6 %collective-permute-start.1 = (bf16[56,4096]{1,0:T(8,128)(2,1)}, bf16[56,4096]{1,0:T(8,128)(2,1)}, u32[]{:S(2)}, u32[]{:S(2)}) collective-permute-start(bf16[56,4096]{1,0:T(8,128)(2,1)} %fusion.3), channel_id=1, source_target_pairs={{3,0},{0,1},{1,2},{2,3},{7,4},{4,5},{5,6},{6,7},{11,8},{8,9},{9,10... | collective-permute-start | bytes 1376264 | tf_op jit(solution)/shard_map/ppermute | solution.py:26
  12.3 0.7 mul.277
  13.0 1.6 %reshape.390 = f32[4,12,4096]{2,1,0:T(8,128)} reshape(f32[1,16,3,2,2048]{4,3,2,1,0:T(2,128)S(1)} %copy-done.1) | data formatting | bytes 1572864 | tf_op jit(solution)/shard_map/reshape | solution.py:31
  14.6 0.7 slice.130
  15.5 0.3 fusion.15
  15.8 0.2 fusion.20
  16.0 1.1 fusion.4
  17.2 0.9 multiply_convert_fusion.2.near_rows_ref
  18.2 0.8 multiply_convert_fusion.1
  18.9 1.5 %pad_maximum_fusion.table_ref = bf16[4096,256]{1,0:T(8,128)(2,1)} fusion(bf16[2048,256]{1,0:T(8,128)(2,1)S(1)} %bitcast.65, bf16[2048,256]{1,0:T(8,128)(2,1)S(1)} %bitcast.64), kind=kLoop, calls=%fused_computation.1 | loop fusion | flops 4194304 | bytes 4194304 | tf_op jit(solution)/shard_map/concatenate | solution.py:59
  20.4 8.3 %shard_map.41.after_ref = f32[2,32,40,256]{3,2,1,0:T(8,128)} custom-call(bf16[4,12,4096]{2,1,0:T(8,128)(2,1)} %multiply_convert_fusion.2.near_rows_ref, bf16[48,4096]{1,0:T(8,128)(2,1)} %copy-done.2, bf16[4096,256]{1,0:T(8,128)(2,1)} %pad_maximum_fusion.table_ref), custom_call_target="tpu_custom_call" | custom-call | tf_op jit(solution)/shard_map/pallas_call | solution.py:123
  28.7 11.6 %collective-permute-done.2 = bf16[56,4096]{1,0:T(8,128)(2,1)} collective-permute-done((bf16[56,4096]{1,0:T(8,128)(2,1)}, bf16[56,4096]{1,0:T(8,128)(2,1)}, u32[]{:S(2)}, u32[]{:S(2)}) %collective-permute-start.2) | collective-permute-done | bytes 458784 | tf_op jit(solution)/shard_map/ppermute | solution.py:26
  40.3 0.7 slice_convert_fusion
  41.1 0.1 reshape.395
  41.6 0.7 fusion.22
  42.7 0.1 copy.18
  42.9 0.7 copy.41
  43.6 0.9 slice_select_fusion.1
  44.6 0.8 reshape.393.far_rows_ref
  45.3 1.8 %slice_select_fusion.far_cols_ref = bf16[48,4096]{1,0:T(8,128)(2,1)} fusion(bf16[48,4096]{1,0:T(8,128)(2,1)S(1)} %copy-done.3, bf16[56,4096]{1,0:T(8,128)(2,1)} %collective-permute-done.2, pred[]{:T(512)S(6)} %lt.33), kind=kLoop, calls=%fused_computation.18 | loop fusion | flops 196608 | bytes 1179649 | tf_op jit(solution)/shard_map/jit(_where)/select_n | solution.py:204
  47.1 1.8 %slice.128.passed_ref = bf16[48,4096]{1,0:T(8,128)(2,1)} slice(bf16[56,4096]{1,0:T(8,128)(2,1)} %collective-permute-done.1), slice={[0:48], [0:4096]} | slice | bytes 786432 | tf_op jit(solution)/shard_map/slice | solution.py:201
  48.9 11.4 %shard_map.42 = f32[2,32,56,256]{3,2,1,0:T(8,128)} custom-call(bf16[4,12,4096]{2,1,0:T(8,128)(2,1)} %multiply_convert_fusion.2.near_rows_ref, bf16[48,4096]{1,0:T(8,128)(2,1)} %slice.128.passed_ref, bf16[4,6,4096]{2,1,0:T(8,128)(2,1)} %reshape.393.far_rows_ref, bf16[48,4096]{1,0:T(8,128)(2,1)} %slice_select_fusion.far_cols_ref, ...), custom_call_target="tpu_custom_call" | custom-call | tf_op jit(solution)/shard_map/pallas_call | solution.py:123
  60.4 3.1 %dynamic-slice_bitcast_fusion = f32[32,56,256]{2,1,0:T(8,128)} fusion(f32[2,32,56,256]{3,2,1,0:T(8,128)} %shard_map.42, s32[]{:T(128)S(6)} %select_n.110), kind=kLoop, calls=%fused_computation.6 | loop fusion | bytes 3670020 | tf_op jit(solution)/shard_map/jit(dynamic_index_in_dim)/squeeze | solution.py:180
  63.4 1.9 %collective-permute-start.3 = (f32[32,56,256]{2,1,0:T(8,128)}, f32[32,56,256]{2,1,0:T(8,128)}, u32[]{:S(2)}, u32[]{:S(2)}) collective-permute-start(f32[32,56,256]{2,1,0:T(8,128)} %dynamic-slice_bitcast_fusion), channel_id=1, source_target_pairs={{0,4},{4,0},{1,5},{5,1},{2,6},{6,2},{3,7},{7,3},{8,12},{12,8},{9,1... | collective-permute-start | bytes 5505032 | tf_op jit(solution)/shard_map/ppermute | solution.py:181
  65.3 1.2 %dynamic-slice_bitcast_fusion.1 = f32[32,40,256]{2,1,0:T(8,128)} fusion(f32[2,32,40,256]{3,2,1,0:T(8,128)S(1)} %copy-done, s32[]{:T(128)S(6)} %select_n.110), kind=kLoop, calls=%fused_computation.10 | loop fusion | bytes 2621444 | tf_op jit(solution)/shard_map/jit(dynamic_index_in_dim)/squeeze | solution.py:180
  66.5 4.5 %collective-permute-done = f32[32,40,256]{2,1,0:T(8,128)} collective-permute-done((f32[32,40,256]{2,1,0:T(8,128)}, f32[32,40,256]{2,1,0:T(8,128)}, u32[]{:S(2)}, u32[]{:S(2)}) %collective-permute-start) | collective-permute-done | bytes 1310752 | tf_op jit(solution)/shard_map/ppermute | solution.py:181
  70.9 1.4 %fusion.1 = bf16[32,40,256]{2,1,0:T(8,128)(2,1)S(1)} fusion(f32[32,40,256]{2,1,0:T(8,128)} %collective-permute-done, f32[2,32,40,256]{3,2,1,0:T(8,128)S(1)} %copy-done, s32[]{:T(128)S(6)} %select_n.109), kind=kLoop, calls=%fused_computation.9 | loop fusion | flops 655360 | bytes 3276804 | tf_op jit(solution)/shard_map/convert.1
  72.4 2.2 %fusion = bf16[32,56,256]{2,1,0:T(8,128)(2,1)S(1)} fusion(f32[32,56,256]{2,1,0:T(8,128)} %collective-permute-done.3, f32[2,32,56,256]{3,2,1,0:T(8,128)} %shard_map.42, s32[]{:T(128)S(6)} %select_n.109), kind=kLoop, calls=%fused_computation.5 | loop fusion | flops 917504 | bytes 4587524 | tf_op jit(solution)/shard_map/convert.2
  74.6 0.2 pad_maximum_fusion.1
  74.8 1.3 %copy.22 = bf16[2,16,96,256]{3,2,0,1:T(8,128)(2,1)} copy(bf16[2,16,96,256]{3,2,1,0:T(8,128)(2,1)S(1)} %bitcast.63) | data formatting | bytes 3145728 | tf_op jit(solution)/shard_map/convert_element_type | solution.py:245
  76.1 6.8 %all-to-all-start = ((bf16[2,16,96,256]{3,2,0,1:T(8,128)(2,1)}), bf16[2,16,96,256]{3,2,0,1:T(8,128)(2,1)S(1)}, u32[]{:S(2)}, u32[]{:S(2)}) async-start(bf16[2,16,96,256]{3,2,0,1:T(8,128)(2,1)} %copy.22), calls=%async_computation | async-start | bytes 3145728 | tf_op jit(solution)/shard_map/all_to_all | solution.py:246
  82.8 22.3 %all-to-all-done = bf16[2,16,96,256]{3,2,0,1:T(8,128)(2,1)S(1)} async-done(((bf16[2,16,96,256]{3,2,0,1:T(8,128)(2,1)}), bf16[2,16,96,256]{3,2,0,1:T(8,128)(2,1)S(1)}, u32[]{:S(2)}, u32[]{:S(2)}) %all-to-all-start) | async-done | bytes 1572896 | tf_op jit(solution)/shard_map/all_to_all | solution.py:246
  105.1 0.2 convert_reduce_fusion
  105.3 6.4 %collective-permute-start.4 = (f32[96,256]{1,0:T(8,128)S(1)}, f32[96,256]{1,0:T(8,128)S(1)}, u32[]{:S(2)}, u32[]{:S(2)}) collective-permute-start(f32[96,256]{1,0:T(8,128)S(1)} %select_bitcast_fusion), channel_id=1, source_target_pairs={{0,128},{128,0},{1,129},{129,1},{2,130},{130,2},{3,131},{131,3},{4... | collective-permute-start | bytes 294920 | tf_op jit(solution)/shard_map/ppermute | solution.py:251
  111.7 2.0 %collective-permute-done.4 = f32[96,256]{1,0:T(8,128)S(1)} collective-permute-done((f32[96,256]{1,0:T(8,128)S(1)}, f32[96,256]{1,0:T(8,128)S(1)}, u32[]{:S(2)}, u32[]{:S(2)}) %collective-permute-start.4) | collective-permute-done | bytes 98336 | tf_op jit(solution)/shard_map/ppermute | solution.py:251
  114.1 0.7 copy.23
  114.7 0.6 broadcast_in_dim.14
  (50 shorter events, 1.8 us)
Async XLA Ops:
  4.1 1.3 %copy-start.1 = (f32[1,16,3,2,2048]{4,3,2,1,0:T(2,128)S(1)}, f32[1,16,3,2,2048]{4,3,2,1,0:T(2,128)}, u32[]{:S(2)}) copy-start(f32[1,16,3,2,2048]{4,3,2,1,0:T(2,128)} %param.6) | copy-start | bytes 2359300
  6.0 8.6 %copy-start.2 = (bf16[48,4096]{1,0:T(8,128)(2,1)}, bf16[48,4096]{1,0:T(8,128)(2,1)S(1)}, u32[]{:S(2)}) copy-start(bf16[48,4096]{1,0:T(8,128)(2,1)S(1)} %multiply_convert_fusion.3.own_ref) | copy-start | bytes 1179652
  6.9 33.4 %collective-permute-start.2 = (bf16[56,4096]{1,0:T(8,128)(2,1)}, bf16[56,4096]{1,0:T(8,128)(2,1)}, u32[]{:S(2)}, u32[]{:S(2)}) collective-permute-start(bf16[56,4096]{1,0:T(8,128)(2,1)} %fusion.3), channel_id=1, source_target_pairs={{2,0},{3,1},{0,2},{1,3},{6,4},{7,5},{4,6},{5,7},{10,8},{11,9},{8,1... | collective-permute-start | bytes 1376264 | tf_op jit(solution)/shard_map/ppermute | solution.py:26
  10.7 30.9 %collective-permute-start.1 = (bf16[56,4096]{1,0:T(8,128)(2,1)}, bf16[56,4096]{1,0:T(8,128)(2,1)}, u32[]{:S(2)}, u32[]{:S(2)}) collective-permute-start(bf16[56,4096]{1,0:T(8,128)(2,1)} %fusion.3), channel_id=1, source_target_pairs={{3,0},{0,1},{1,2},{2,3},{7,4},{4,5},{5,6},{6,7},{11,8},{8,9},{9,10... | collective-permute-start | bytes 1376264 | tf_op jit(solution)/shard_map/ppermute | solution.py:26
  15.3 1.9 %copy-start.4 = (f32[4,12,4096]{2,1,0:T(8,128)S(1)}, f32[4,12,4096]{2,1,0:T(8,128)}, u32[]{:S(2)}) copy-start(f32[4,12,4096]{2,1,0:T(8,128)} %reshape.390) | copy-start | bytes 2359300
  28.7 16.6 %copy-start.3 = (bf16[48,4096]{1,0:T(8,128)(2,1)S(1)}, bf16[48,4096]{1,0:T(8,128)(2,1)}, u32[]{:S(2)}) copy-start(bf16[48,4096]{1,0:T(8,128)(2,1)} %copy-done.2) | copy-start | bytes 1179652
  60.4 4.9 %copy-start = (f32[2,32,40,256]{3,2,1,0:T(8,128)S(1)}, f32[2,32,40,256]{3,2,1,0:T(8,128)}, u32[]{:S(2)}) copy-start(f32[2,32,40,256]{3,2,1,0:T(8,128)} %shard_map.41.after_ref) | copy-start | bytes 7864324
  63.4 8.9 %collective-permute-start.3 = (f32[32,56,256]{2,1,0:T(8,128)}, f32[32,56,256]{2,1,0:T(8,128)}, u32[]{:S(2)}, u32[]{:S(2)}) collective-permute-start(f32[32,56,256]{2,1,0:T(8,128)} %dynamic-slice_bitcast_fusion), channel_id=1, source_target_pairs={{0,4},{4,0},{1,5},{5,1},{2,6},{6,2},{3,7},{7,3},{8,12},{12,8},{9,1... | collective-permute-start | bytes 5505032 | tf_op jit(solution)/shard_map/ppermute | solution.py:181
  66.5 4.5 %collective-permute-start = (f32[32,40,256]{2,1,0:T(8,128)}, f32[32,40,256]{2,1,0:T(8,128)}, u32[]{:S(2)}, u32[]{:S(2)}) collective-permute-start(f32[32,40,256]{2,1,0:T(8,128)} %dynamic-slice_bitcast_fusion.1), channel_id=1, source_target_pairs={{0,4},{4,0},{1,5},{5,1},{2,6},{6,2},{3,7},{7,3},{8,12},{12,8},{9,1... | collective-permute-start | bytes 3932168 | tf_op jit(solution)/shard_map/ppermute | solution.py:181
  76.1 29.0 %all-to-all-start = ((bf16[2,16,96,256]{3,2,0,1:T(8,128)(2,1)}), bf16[2,16,96,256]{3,2,0,1:T(8,128)(2,1)S(1)}, u32[]{:S(2)}, u32[]{:S(2)}) async-start(bf16[2,16,96,256]{3,2,0,1:T(8,128)(2,1)} %copy.22), calls=%async_computation | async-start | bytes 3145728 | tf_op jit(solution)/shard_map/all_to_all | solution.py:246
  105.3 8.4 %collective-permute-start.4 = (f32[96,256]{1,0:T(8,128)S(1)}, f32[96,256]{1,0:T(8,128)S(1)}, u32[]{:S(2)}, u32[]{:S(2)}) collective-permute-start(f32[96,256]{1,0:T(8,128)S(1)} %select_bitcast_fusion), channel_id=1, source_target_pairs={{0,128},{128,0},{1,129},{129,1},{2,130},{130,2},{3,131},{131,3},{4... | collective-permute-start | bytes 294920 | tf_op jit(solution)/shard_map/ppermute | solution.py:251
